TPU v7x, 512 devices: a whole 4x8x8 slice. The times are simulated.
512 devices in a mesh: param: 32 (over x, z), ex: 16 (over y, core).
Axes of the slice: x: 4, y: 8, z: 8, core: 2. Of those that a mesh axis runs over, the one named last changes fastest.
Arguments:
- adapter_gradients: bfloat16 [512, 131072], P('ex', 'param'), may hold values from -560 to 560
- sign_hash_keys: int32 [4], replicated, may hold values from 1 to 16777215
- target_indices: int32 [256], replicated, may hold values from 0 to 511
Outputs:
- features: float32 [512, 8192], P('ex', 'param')
- scores: float32 [512, 256], P('ex')
All inputs are finite; a program needn't handle non-finite values.
Results may differ from a plain program's by a relative error of at most 0.0003.
Values sent between devices are 32-bit elements; how exact they have to be, the bound alone decides.
No kernel may reach another device: no remote copies, remote signals or barrier semaphores. Data moves between devices by JAX's collectives and lax.ppermute only.
A program may use at most 128 MiB of HBM per device.

v0:
```python
import jax
import jax.numpy as jnp
from jax import lax
from jax.sharding import PartitionSpec as P

K = 8192
norm_eps = 1e-06


def sign_block(sign_hash_keys, first_row, row_count, col_count):
    mult_row = sign_hash_keys[0] | 1
    mult_col = sign_hash_keys[1] | 1
    seed_add = sign_hash_keys[2]
    mix_mult = sign_hash_keys[3] | 1
    row_ids = first_row + lax.iota(jnp.int32, row_count)[:, None]
    col_ids = lax.iota(jnp.int32, col_count)[None, :]
    hashed = row_ids * mult_row + col_ids * mult_col + seed_add
    hashed = hashed ^ lax.shift_right_logical(hashed, jnp.full_like(hashed, 16))
    hashed = hashed * mix_mult
    hashed = hashed ^ lax.shift_right_logical(hashed, jnp.full_like(hashed, 13))
    hashed = hashed * jnp.int32(-1028477387)
    hashed = hashed ^ lax.shift_right_logical(hashed, jnp.full_like(hashed, 16))
    return jnp.where(hashed < 0, 1.0, -1.0).astype(jnp.bfloat16)


def local(adapter_gradients, sign_hash_keys, target_indices):
    resident_example, resident_rows = adapter_gradients.shape
    row_base = lax.axis_index("param") * jnp.int32(resident_rows)
    turn_count = 8
    rows_per_tile = resident_rows // turn_count
    scale_k = jnp.float32(K)

    def accumulate(tile_idx, totals):
        start_offset = tile_idx * jnp.int32(rows_per_tile)
        gradient_slab = lax.dynamic_slice_in_dim(adapter_gradients, start_offset, rows_per_tile, 1)
        signs = sign_block(sign_hash_keys, row_base + start_offset, rows_per_tile, K)
        return totals + jnp.dot(gradient_slab, signs, preferred_element_type=jnp.float32)

    partial_sums = lax.fori_loop(
        jnp.int32(0),
        jnp.int32(turn_count),
        accumulate,
        jnp.zeros((resident_example, K), jnp.float32),
    )
    projected = lax.psum_scatter(partial_sums, "param", scatter_dimension=1, tiled=True)
    own_squares = jnp.sum(projected * projected, axis=1)
    total_sq = lax.psum(own_squares, "param")
    features = projected * jnp.sqrt(scale_k / (total_sq + norm_eps))[:, None]
    pool_rows = lax.all_gather(features, "ex", axis=0, tiled=True)
    targets = jnp.take(pool_rows, target_indices, axis=0)
    partial_dots = jnp.dot(features, targets.T, precision=lax.Precision.HIGHEST)
    scores = lax.psum(partial_dots, "param") / scale_k
    return (features, scores)


def solution(mesh):
    return jax.shard_map(
        local,
        mesh=mesh,
        in_specs=(P("ex", "param"), P(), P()),
        out_specs=(P("ex", "param"), P("ex", None)),
        check_vma=False,
    )
```

profile of v0, /device:TPU:8, one launch (start us, length us, event | category | flops | bytes accessed | tf_op | source)
XLA Modules:
  0.0 555.2 jit_solution(16775991105922428957)
XLA Ops:
  7.2 0.0 reduce-scatter.2.cloned.1.call-start
  7.2 1.4 fusion.24
  10.4 81.0 %while.12 = (s32[]{:T(128)}, f32[32,8192]{1,0:T(8,128)S(1)}, bf16[32,4096]{1,0:T(8,128)(2,1)}, s32[]{:T(128)}, s32[]{:T(128)}, /*index=5*/s32[]{:T(128)}, s32[4]...) while((s32[]{:T(128)}, f32[32,8192]{1,0:T(8,128)S(1)}, ...), condition=%wide.region_1.2_spmd.clone, body=%wide.region_0.1_spmd.clone.sunk | while | flops 323494912 | bytes 2200785 | solution.py:39
  10.5 1.3 slice.29
  11.8 8.8 %convolution_add_fusion.2 = f32[32,8192]{1,0:T(8,128)S(1)} fusion(s32[]{:T(128)} %get-tuple-element.187, s32[]{:T(128)} %bitcast.6, s32[8192]{0:T(1024)S(1)} %iota_multiply_fusion.2, s32[512]{0:T(512)S(1)} %add_multiply_fusion.2, f32[32,8192]{1,0:T(8,128)S(1)} %get-tuple-element.169, pred[]{:T(512)S(6)} %compare.3, ...), kind=kOutput, calls=%fused_computation.8.clone.1 | convolution fusion | flops 323485696 | bytes 2165765 | tf_op jit(solution)/shard_map/while/body/dot_general | solution.py:37
  20.6 1.3 slice.29
  21.9 8.8 %convolution_add_fusion.2 = f32[32,8192]{1,0:T(8,128)S(1)} fusion(s32[]{:T(128)} %get-tuple-element.187, s32[]{:T(128)} %bitcast.6, s32[8192]{0:T(1024)S(1)} %iota_multiply_fusion.2, s32[512]{0:T(512)S(1)} %add_multiply_fusion.2, f32[32,8192]{1,0:T(8,128)S(1)} %get-tuple-element.169, pred[]{:T(512)S(6)} %compare.3, ...), kind=kOutput, calls=%fused_computation.8.clone.1 | convolution fusion | flops 323485696 | bytes 2165765 | tf_op jit(solution)/shard_map/while/body/dot_general | solution.py:37
  30.8 1.3 slice.29
  32.1 8.8 %convolution_add_fusion.2 = f32[32,8192]{1,0:T(8,128)S(1)} fusion(s32[]{:T(128)} %get-tuple-element.187, s32[]{:T(128)} %bitcast.6, s32[8192]{0:T(1024)S(1)} %iota_multiply_fusion.2, s32[512]{0:T(512)S(1)} %add_multiply_fusion.2, f32[32,8192]{1,0:T(8,128)S(1)} %get-tuple-element.169, pred[]{:T(512)S(6)} %compare.3, ...), kind=kOutput, calls=%fused_computation.8.clone.1 | convolution fusion | flops 323485696 | bytes 2165765 | tf_op jit(solution)/shard_map/while/body/dot_general | solution.py:37
  40.9 1.3 slice.29
  42.2 8.8 %convolution_add_fusion.2 = f32[32,8192]{1,0:T(8,128)S(1)} fusion(s32[]{:T(128)} %get-tuple-element.187, s32[]{:T(128)} %bitcast.6, s32[8192]{0:T(1024)S(1)} %iota_multiply_fusion.2, s32[512]{0:T(512)S(1)} %add_multiply_fusion.2, f32[32,8192]{1,0:T(8,128)S(1)} %get-tuple-element.169, pred[]{:T(512)S(6)} %compare.3, ...), kind=kOutput, calls=%fused_computation.8.clone.1 | convolution fusion | flops 323485696 | bytes 2165765 | tf_op jit(solution)/shard_map/while/body/dot_general | solution.py:37
  51.0 1.3 slice.29
  52.3 8.8 %convolution_add_fusion.2 = f32[32,8192]{1,0:T(8,128)S(1)} fusion(s32[]{:T(128)} %get-tuple-element.187, s32[]{:T(128)} %bitcast.6, s32[8192]{0:T(1024)S(1)} %iota_multiply_fusion.2, s32[512]{0:T(512)S(1)} %add_multiply_fusion.2, f32[32,8192]{1,0:T(8,128)S(1)} %get-tuple-element.169, pred[]{:T(512)S(6)} %compare.3, ...), kind=kOutput, calls=%fused_computation.8.clone.1 | convolution fusion | flops 323485696 | bytes 2165765 | tf_op jit(solution)/shard_map/while/body/dot_general | solution.py:37
  61.1 1.3 slice.29
  62.4 8.8 %convolution_add_fusion.2 = f32[32,8192]{1,0:T(8,128)S(1)} fusion(s32[]{:T(128)} %get-tuple-element.187, s32[]{:T(128)} %bitcast.6, s32[8192]{0:T(1024)S(1)} %iota_multiply_fusion.2, s32[512]{0:T(512)S(1)} %add_multiply_fusion.2, f32[32,8192]{1,0:T(8,128)S(1)} %get-tuple-element.169, pred[]{:T(512)S(6)} %compare.3, ...), kind=kOutput, calls=%fused_computation.8.clone.1 | convolution fusion | flops 323485696 | bytes 2165765 | tf_op jit(solution)/shard_map/while/body/dot_general | solution.py:37
  71.3 1.3 slice.29
  72.6 8.8 %convolution_add_fusion.2 = f32[32,8192]{1,0:T(8,128)S(1)} fusion(s32[]{:T(128)} %get-tuple-element.187, s32[]{:T(128)} %bitcast.6, s32[8192]{0:T(1024)S(1)} %iota_multiply_fusion.2, s32[512]{0:T(512)S(1)} %add_multiply_fusion.2, f32[32,8192]{1,0:T(8,128)S(1)} %get-tuple-element.169, pred[]{:T(512)S(6)} %compare.3, ...), kind=kOutput, calls=%fused_computation.8.clone.1 | convolution fusion | flops 323485696 | bytes 2165765 | tf_op jit(solution)/shard_map/while/body/dot_general | solution.py:37
  81.4 1.3 slice.29
  82.7 8.8 %convolution_add_fusion.2 = f32[32,8192]{1,0:T(8,128)S(1)} fusion(s32[]{:T(128)} %get-tuple-element.187, s32[]{:T(128)} %bitcast.6, s32[8192]{0:T(1024)S(1)} %iota_multiply_fusion.2, s32[512]{0:T(512)S(1)} %add_multiply_fusion.2, f32[32,8192]{1,0:T(8,128)S(1)} %get-tuple-element.169, pred[]{:T(512)S(6)} %compare.3, ...), kind=kOutput, calls=%fused_computation.8.clone.1 | convolution fusion | flops 323485696 | bytes 2165765 | tf_op jit(solution)/shard_map/while/body/dot_general | solution.py:37
  91.5 0.0 copy-start
  91.5 0.0 copy-start.2
  91.5 1.0 copy-done
  92.5 0.0 reduce-scatter.2.cloned.1.call-update
  92.5 0.0 copy-done.2
  92.5 225.0 %reduce-scatter.2.cloned.1.call-done = f32[32,256]{1,0:T(8,128)} async-done(((f32[32,8192]{1,0:T(8,128)}), f32[32,256]{1,0:T(8,128)}) %reduce-scatter.2.cloned.1.call-update) | async-done | bytes 32784 | tf_op jit(solution)/shard_map/reduce_scatter | solution.py:45
  317.6 0.9 multiply_reduce_fusion
  318.4 72.3 %psum.14 = f32[32]{0:T(128)S(1)} all-reduce(f32[32]{0:T(128)S(1)} %multiply_reduce_fusion), channel_id=1, replica_groups=mesh['param'=32,'ex'=16] {'param'}, use_global_device_ids=true, to_apply=%region_4.5 | all-reduce | flops 32 | bytes 256 | tf_op jit(solution)/shard_map/psum | solution.py:47
  390.7 0.8 broadcast_multiply_fusion.1
  391.5 0.0 copy-start.1
  391.5 17.1 %all_gather.3 = f32[512,256]{1,0:T(8,128)S(1)} all-gather(f32[32,256]{1,0:T(8,128)S(1)} %broadcast_multiply_fusion.1), channel_id=1, replica_groups=mesh['param'=32,'ex'=16] {'ex'}, dimensions={0}, use_global_device_ids=true | all-gather | bytes 557056 | tf_op jit(solution)/shard_map/all_gather | solution.py:49
  408.7 1.0 gather_fusion
  409.6 0.0 copy-done.1
  409.6 0.4 fusion.19
  410.1 137.7 %psum.15 = f32[32,256]{1,0:T(8,128)S(1)} all-reduce(f32[32,256]{1,0:T(8,128)S(1)} %fusion.19), channel_id=1, replica_groups=mesh['param'=32,'ex'=16] {'param'}, use_global_device_ids=true, to_apply=%region_5.6 | all-reduce | flops 8192 | bytes 65536 | tf_op jit(solution)/shard_map/psum | solution.py:52
  547.7 0.6 broadcast_multiply_fusion
  (21 shorter events, 0.2 us)
Async XLA Ops:
  7.2 310.4 %reduce-scatter.2.cloned.1.call-start = ((), (), s32[]{:S(2)}) async-start(), calls=%async_computation.1 | async-start | bytes 1081344 | tf_op jit(solution)/shard_map/reduce_scatter | solution.py:45
  91.5 1.0 copy-start
  91.5 1.0 copy-start.2
  391.5 18.1 %copy-start.1 = (f32[32,256]{1,0:T(8,128)}, f32[32,256]{1,0:T(8,128)S(1)}, u32[]{:S(2)}) copy-start(f32[32,256]{1,0:T(8,128)S(1)} %broadcast_multiply_fusion.1) | copy-start | bytes 98308
Sparse Core Ops, SparseCore 0:
  92.6 224.9 reduce-scatter.1
where the time goes:
time: 556 us; the launch traced here: 555 us
  blocking collectives  227 us (41%)
  waiting for transfers between devices  225 us (40%)
  matrix products  70.5 us (13%)
  between operations  16 us (3%)
  local copies, waits for them, and re-layouts  13.7 us (2%)
    reduce_scatter x1, waiting for transfers between devices, local(): lax.psum_scatter(partial_sums, 'param', scatter_dimension=1, tiled=True)  225 us
    psum x1, blocking collectives, local(): scores = lax.psum(partial_dots, 'param') / scale_k  138 us
    psum x1, blocking collectives, local(): total_sq = lax.psum(own_squares, 'param')  72.3 us
    dot_general x8, matrix products, accumulate(): jnp.dot(gradient_slab, signs, preferred_element_type=jnp.float32)  70 us
    all_gather x1, blocking collectives, local(): pool_rows = lax.all_gather(features, 'ex', axis=0, tiled=True)  17.1 us
  transfers between devices with their start and end apart: 1, of which 1 were waited for; matrix products, arithmetic and copies ran while one was open for 0% of the time, Pallas kernels for 0%

commit v1 on v0

--- a/solution.py
+++ b/solution.py
@@ -2,6 +2,7 @@
 import jax.numpy as jnp
 from jax import lax
 from jax.sharding import PartitionSpec as P
+from jax.lax import axis_index, axis_size, ppermute
 
 K = 8192
 norm_eps = 1e-06
@@ -46,7 +47,19 @@
     own_squares = jnp.sum(projected * projected, axis=1)
     total_sq = lax.psum(own_squares, "param")
     features = projected * jnp.sqrt(scale_k / (total_sq + norm_eps))[:, None]
-    pool_rows = lax.all_gather(features, "ex", axis=0, tiled=True)
+
+    def build_layers_all_in(array_here):
+        fan = axis_size("ex")
+        u = 0
+        store = [array_here]
+        while u < fan - 1:
+            small = ppermute(store[-1], "ex", [(t, (t + 1) % fan) for t in range(fan)])
+            store.append(small)
+            u += 1
+        top = jnp.concatenate(store[::-1], axis=0)
+        return jnp.roll(top, shift=(axis_index("ex") + 1) * array_here.shape[0], axis=0)
+
+    pool_rows = build_layers_all_in(features)
     targets = jnp.take(pool_rows, target_indices, axis=0)
     partial_dots = jnp.dot(features, targets.T, precision=lax.Precision.HIGHEST)
     scores = lax.psum(partial_dots, "param") / scale_k

time: 556 us -> 608 us (1.094)
  the two profiles are of different devices: /device:TPU:8 before, /device:TPU:32 now
where the time goes in v1:
time: 608 us; the launch traced here: 607 us
  waiting for transfers between devices  293 us (48%)
  blocking collectives  210 us (35%)
  matrix products  70.4 us (12%)
  between operations  16.2 us (3%)
  local copies, waits for them, and re-layouts  13.9 us (2%)
    reduce_scatter x1, waiting for transfers between devices, local(): lax.psum_scatter(partial_sums, 'param', scatter_dimension=1, tiled=True)  225 us
    psum x1, blocking collectives, local(): scores = lax.psum(partial_dots, 'param') / scale_k  138 us
    psum x1, blocking collectives, local(): total_sq = lax.psum(own_squares, 'param')  72.2 us
    dot_general x8, matrix products, accumulate(): jnp.dot(gradient_slab, signs, preferred_element_type=jnp.float32)  70 us
    ppermute x15, waiting for transfers between devices, build_layers_all_in(): small = ppermute(store[-1], 'ex', [(t, (t + 1) % fan) for t in range(fan)])  68.2 us
  transfers between devices with their start and end apart: 16, of which 16 were waited for; matrix products, arithmetic and copies ran while one was open for 0% of the time, Pallas kernels for 0%

profile of v1, /device:TPU:32, one launch (start us, length us, event | category | flops | bytes accessed | tf_op | source)
XLA Modules:
  0.0 606.6 jit_solution(7384862253227043903)
XLA Ops:
  7.2 0.0 reduce-scatter.2.cloned.1.call-start
  7.2 1.4 fusion.24
  10.4 80.9 %while.12 = (s32[]{:T(128)}, f32[32,8192]{1,0:T(8,128)S(1)}, bf16[32,4096]{1,0:T(8,128)(2,1)}, s32[]{:T(128)}, s32[]{:T(128)}, /*index=5*/s32[]{:T(128)}, s32[4]...) while((s32[]{:T(128)}, f32[32,8192]{1,0:T(8,128)S(1)}, ...), condition=%wide.region_1.2_spmd.clone, body=%wide.region_0.1_spmd.clone.sunk | while | flops 323494912 | bytes 2200785 | solution.py:40
  10.5 1.3 slice.29
  11.8 8.7 %convolution_add_fusion.2 = f32[32,8192]{1,0:T(8,128)S(1)} fusion(s32[]{:T(128)} %get-tuple-element.187, s32[]{:T(128)} %bitcast.6, s32[8192]{0:T(1024)S(1)} %iota_multiply_fusion.2, s32[512]{0:T(512)S(1)} %add_multiply_fusion.2, f32[32,8192]{1,0:T(8,128)S(1)} %get-tuple-element.169, pred[]{:T(512)S(6)} %compare.4, ...), kind=kOutput, calls=%fused_computation.8.clone.1 | convolution fusion | flops 323485696 | bytes 2165765 | tf_op jit(solution)/shard_map/while/body/dot_general | solution.py:38
  20.6 1.3 slice.29
  21.9 8.7 %convolution_add_fusion.2 = f32[32,8192]{1,0:T(8,128)S(1)} fusion(s32[]{:T(128)} %get-tuple-element.187, s32[]{:T(128)} %bitcast.6, s32[8192]{0:T(1024)S(1)} %iota_multiply_fusion.2, s32[512]{0:T(512)S(1)} %add_multiply_fusion.2, f32[32,8192]{1,0:T(8,128)S(1)} %get-tuple-element.169, pred[]{:T(512)S(6)} %compare.4, ...), kind=kOutput, calls=%fused_computation.8.clone.1 | convolution fusion | flops 323485696 | bytes 2165765 | tf_op jit(solution)/shard_map/while/body/dot_general | solution.py:38
  30.7 1.3 slice.29
  32.0 8.7 %convolution_add_fusion.2 = f32[32,8192]{1,0:T(8,128)S(1)} fusion(s32[]{:T(128)} %get-tuple-element.187, s32[]{:T(128)} %bitcast.6, s32[8192]{0:T(1024)S(1)} %iota_multiply_fusion.2, s32[512]{0:T(512)S(1)} %add_multiply_fusion.2, f32[32,8192]{1,0:T(8,128)S(1)} %get-tuple-element.169, pred[]{:T(512)S(6)} %compare.4, ...), kind=kOutput, calls=%fused_computation.8.clone.1 | convolution fusion | flops 323485696 | bytes 2165765 | tf_op jit(solution)/shard_map/while/body/dot_general | solution.py:38
  40.8 1.3 slice.29
  42.1 8.7 %convolution_add_fusion.2 = f32[32,8192]{1,0:T(8,128)S(1)} fusion(s32[]{:T(128)} %get-tuple-element.187, s32[]{:T(128)} %bitcast.6, s32[8192]{0:T(1024)S(1)} %iota_multiply_fusion.2, s32[512]{0:T(512)S(1)} %add_multiply_fusion.2, f32[32,8192]{1,0:T(8,128)S(1)} %get-tuple-element.169, pred[]{:T(512)S(6)} %compare.4, ...), kind=kOutput, calls=%fused_computation.8.clone.1 | convolution fusion | flops 323485696 | bytes 2165765 | tf_op jit(solution)/shard_map/while/body/dot_general | solution.py:38
  51.0 1.3 slice.29
  52.3 8.7 %convolution_add_fusion.2 = f32[32,8192]{1,0:T(8,128)S(1)} fusion(s32[]{:T(128)} %get-tuple-element.187, s32[]{:T(128)} %bitcast.6, s32[8192]{0:T(1024)S(1)} %iota_multiply_fusion.2, s32[512]{0:T(512)S(1)} %add_multiply_fusion.2, f32[32,8192]{1,0:T(8,128)S(1)} %get-tuple-element.169, pred[]{:T(512)S(6)} %compare.4, ...), kind=kOutput, calls=%fused_computation.8.clone.1 | convolution fusion | flops 323485696 | bytes 2165765 | tf_op jit(solution)/shard_map/while/body/dot_general | solution.py:38
  61.1 1.3 slice.29
  62.4 8.7 %convolution_add_fusion.2 = f32[32,8192]{1,0:T(8,128)S(1)} fusion(s32[]{:T(128)} %get-tuple-element.187, s32[]{:T(128)} %bitcast.6, s32[8192]{0:T(1024)S(1)} %iota_multiply_fusion.2, s32[512]{0:T(512)S(1)} %add_multiply_fusion.2, f32[32,8192]{1,0:T(8,128)S(1)} %get-tuple-element.169, pred[]{:T(512)S(6)} %compare.4, ...), kind=kOutput, calls=%fused_computation.8.clone.1 | convolution fusion | flops 323485696 | bytes 2165765 | tf_op jit(solution)/shard_map/while/body/dot_general | solution.py:38
  71.2 1.3 slice.29
  72.5 8.7 %convolution_add_fusion.2 = f32[32,8192]{1,0:T(8,128)S(1)} fusion(s32[]{:T(128)} %get-tuple-element.187, s32[]{:T(128)} %bitcast.6, s32[8192]{0:T(1024)S(1)} %iota_multiply_fusion.2, s32[512]{0:T(512)S(1)} %add_multiply_fusion.2, f32[32,8192]{1,0:T(8,128)S(1)} %get-tuple-element.169, pred[]{:T(512)S(6)} %compare.4, ...), kind=kOutput, calls=%fused_computation.8.clone.1 | convolution fusion | flops 323485696 | bytes 2165765 | tf_op jit(solution)/shard_map/while/body/dot_general | solution.py:38
  81.3 1.3 slice.29
  82.6 8.7 %convolution_add_fusion.2 = f32[32,8192]{1,0:T(8,128)S(1)} fusion(s32[]{:T(128)} %get-tuple-element.187, s32[]{:T(128)} %bitcast.6, s32[8192]{0:T(1024)S(1)} %iota_multiply_fusion.2, s32[512]{0:T(512)S(1)} %add_multiply_fusion.2, f32[32,8192]{1,0:T(8,128)S(1)} %get-tuple-element.169, pred[]{:T(512)S(6)} %compare.4, ...), kind=kOutput, calls=%fused_computation.8.clone.1 | convolution fusion | flops 323485696 | bytes 2165765 | tf_op jit(solution)/shard_map/while/body/dot_general | solution.py:38
  91.4 0.0 copy-start
  91.4 0.0 copy-start.3
  91.4 1.0 copy-done
  92.3 0.0 reduce-scatter.2.cloned.1.call-update
  92.4 224.8 %reduce-scatter.2.cloned.1.call-done = f32[32,256]{1,0:T(8,128)} async-done(((f32[32,8192]{1,0:T(8,128)}), f32[32,256]{1,0:T(8,128)}) %reduce-scatter.2.cloned.1.call-update) | async-done | bytes 32784 | tf_op jit(solution)/shard_map/reduce_scatter | solution.py:46
  317.2 0.9 multiply_reduce_fusion
  318.1 72.2 %psum.14 = f32[32]{0:T(128)S(1)} all-reduce(f32[32]{0:T(128)S(1)} %multiply_reduce_fusion), channel_id=1, replica_groups=mesh['param'=32,'ex'=16] {'param'}, use_global_device_ids=true, to_apply=%region_4.5 | all-reduce | flops 32 | bytes 256 | tf_op jit(solution)/shard_map/psum | solution.py:48
  390.4 0.8 broadcast_multiply_fusion.1
  391.2 0.0 collective-permute-start
  391.2 4.5 collective-permute-done
  395.8 0.0 collective-permute-start.1
  395.8 4.5 collective-permute-done.1
  400.3 0.0 collective-permute-start.2
  400.3 4.5 collective-permute-done.2
  404.9 0.0 collective-permute-start.3
  404.9 4.5 collective-permute-done.3
  409.4 0.0 collective-permute-start.4
  409.4 4.5 collective-permute-done.4
  414.0 0.0 collective-permute-start.5
  414.0 4.5 collective-permute-done.5
  418.5 0.0 collective-permute-start.6
  418.5 4.5 collective-permute-done.6
  423.1 0.0 collective-permute-start.7
  423.1 4.5 collective-permute-done.7
  427.6 0.0 collective-permute-start.8
  427.6 4.5 collective-permute-done.8
  432.2 0.0 collective-permute-start.9
  432.2 4.5 collective-permute-done.9
  436.7 0.0 collective-permute-start.10
  436.7 4.5 collective-permute-done.10
  441.3 0.0 collective-permute-start.11
  441.3 4.5 collective-permute-done.11
  445.8 0.0 collective-permute-start.12
  445.8 0.0 copy-done.3
  445.9 4.5 collective-permute-done.12
  450.4 0.0 collective-permute-start.13
  450.4 4.5 collective-permute-done.13
  454.9 0.0 collective-permute-start.14
  455.0 4.5 collective-permute-done.14
  459.7 0.1 constant_dynamic-update-slice_fusion.16
  459.9 0.1 constant_dynamic-update-slice_fusion
  460.1 1.0 gather_fusion
  461.0 0.4 fusion.19
  461.5 137.7 %psum.15 = f32[32,256]{1,0:T(8,128)S(1)} all-reduce(f32[32,256]{1,0:T(8,128)S(1)} %fusion.19), channel_id=1, replica_groups=mesh['param'=32,'ex'=16] {'param'}, use_global_device_ids=true, to_apply=%region_5.6 | all-reduce | flops 8192 | bytes 65536 | tf_op jit(solution)/shard_map/psum | solution.py:65
  599.2 0.6 broadcast_multiply_fusion
  (56 shorter events, 0.4 us)
Async XLA Ops:
  7.2 310.0 %reduce-scatter.2.cloned.1.call-start = ((), (), s32[]{:S(2)}) async-start(), calls=%async_computation.1 | async-start | bytes 1081344 | tf_op jit(solution)/shard_map/reduce_scatter | solution.py:46
  91.4 1.0 copy-start
  91.4 354.5 %copy-start.3 = (s32[256]{0:T(256)S(1)}, s32[256]{0:T(256)}, u32[]{:S(2)}) copy-start(s32[256]{0:T(256)} %param.7) | copy-start | bytes 3076
  317.2 142.5 %copy-start.1 = (f32[32,256]{1,0:T(8,128)S(1)}, f32[32,256]{1,0:T(8,128)}, u32[]{:S(2)}) copy-start(f32[32,256]{1,0:T(8,128)} %reduce-scatter.2.cloned.1.call-done) | copy-start | bytes 98308
  391.2 69.8 %copy-start.2 = (f32[32,256]{1,0:T(8,128)}, f32[32,256]{1,0:T(8,128)S(1)}, u32[]{:S(2)}) copy-start(f32[32,256]{1,0:T(8,128)S(1)} %broadcast_multiply_fusion.1) | copy-start | bytes 98308
  391.2 4.6 collective-permute-start
  395.8 4.6 collective-permute-start.1
  400.3 4.6 collective-permute-start.2
  404.9 4.6 collective-permute-start.3
  409.4 4.6 collective-permute-start.4
  414.0 4.6 collective-permute-start.5
  418.5 4.6 collective-permute-start.6
  423.1 4.6 collective-permute-start.7
  427.6 4.6 collective-permute-start.8
  432.2 4.6 collective-permute-start.9
  436.7 4.6 collective-permute-start.10
  441.3 4.6 collective-permute-start.11
  445.8 4.6 collective-permute-start.12
  450.4 4.6 collective-permute-start.13
  454.9 4.6 collective-permute-start.14
Sparse Core Ops, SparseCore 0:
  92.5 224.6 reduce-scatter.1
